TPU v7x, 256 devices: a whole 4x4x8 slice. The times are simulated.
256 devices in a mesh: depth: 16 (over y, z_hi), chan: 16 (over x, z_lo, core).
Axes of the slice: x: 4, y: 4, z: 8 (z_hi: 4, z_lo: 2; z = z_hi * 2 + z_lo), core: 2. Of those that a mesh axis runs over, the one named last changes fastest.
Arguments:
- volume: bfloat16 [256, 16, 4096], P('chan', 'depth'), may hold values from -6 to 6
- w_first: bfloat16 [27, 256, 256], P(None, 'chan'), may hold values from -0.078125 to 0.078125
- b_first: float32 [256], P('chan'), may hold values from -3 to 3
- w_second: bfloat16 [27, 256, 256], P(None, None, 'chan'), may hold values from -0.078125 to 0.078125
- b_second: float32 [256], P('chan'), may hold values from -3 to 3
Outputs:
- block_out: bfloat16 [256, 16, 4096], P('chan', 'depth')
All inputs are finite; a program needn't handle non-finite values.
Results may differ from a plain program's by a relative error of at most 0.0043.
Values may be sent and summed in bfloat16 or wider, within the bound.
No kernel may reach another device: no remote copies, remote signals or barrier semaphores. Data moves between devices by JAX's collectives and lax.ppermute only.
A program may use at most 128 MiB of HBM per device.

v0:
```python
import jax
import jax.numpy as jnp
from jax import lax
from jax.sharding import PartitionSpec as P

W = 64


def extended(array, sides, width):
    for axis, dim in sides:
        peers, length = (lax.axis_size(axis), array.shape[dim])
        up = [(i, (i + 1) % peers) for i in range(peers - 1)]
        down = [(j, i) for i, j in up]
        last = lax.slice_in_dim(array, length - width, length, axis=dim)
        leading = lax.slice_in_dim(array, 0, width, axis=dim)
        before = lax.ppermute(last, axis, up)
        after = lax.ppermute(leading, axis, down)
        array = jnp.concatenate([before, array, after], axis=dim)
    return array


def pad_cells(source):
    return jnp.pad(source, ((0, 0), (0, 0), (W + 1, W + 1)))


def nine_taps(segment):
    seg_chan, planes, cell_count = segment.shape
    padded = pad_cells(segment)
    column = jnp.arange(cell_count) % W
    left_ok = column >= 1
    right_ok = column < W - 1
    per_plane = []
    for plane in range(planes):
        windows = []
        for row_tap in range(3):
            for col_tap in range(3):
                begin = row_tap * W + col_tap
                window = padded[:, plane, begin : begin + cell_count]
                if col_tap == 0:
                    window = jnp.where(left_ok, window, jnp.zeros_like(window))
                elif col_tap == 2:
                    window = jnp.where(right_ok, window, jnp.zeros_like(window))
                windows.append(window)
        per_plane.append(jnp.concatenate(windows, 0))
    return jnp.concatenate(per_plane, 1)


def fold_planes(filters, running, segment):
    seg_chan, padded_depth, cell_count = segment.shape
    slab_depth = padded_depth - 2
    out_chan = filters.shape[2]
    grouped = filters.reshape(3, 9 * seg_chan, out_chan)
    columns = nine_taps(segment)
    total = running
    for depth_tap in range(3):
        window = columns[:, depth_tap * cell_count : (depth_tap + slab_depth) * cell_count]
        total = total + lax.dot_general(
            grouped[depth_tap], window, (((0,), (0,)), ((), ())), preferred_element_type=jnp.float32
        )
    return total


def tap_columns(rimmed):
    chan_local, padded_depth, cell_count = rimmed.shape
    padded = pad_cells(rimmed)
    column = jnp.arange(cell_count) % W
    left_ok = column >= 1
    right_ok = column < W - 1
    gathered_taps = []
    for depth_tap in range(3):
        for row_tap in range(3):
            for col_tap in range(3):
                begin = row_tap * W + col_tap
                window = padded[:, depth_tap, begin : begin + cell_count]
                if col_tap == 0:
                    window = jnp.where(left_ok, window, jnp.zeros_like(window))
                elif col_tap == 2:
                    window = jnp.where(right_ok, window, jnp.zeros_like(window))
                gathered_taps.append(window)
    per_plane = [jnp.concatenate(gathered_taps, 0)]
    return per_plane


def body(volume, w_first, b_first, w_second, b_second):
    chan_local, slab_depth, cell_count = volume.shape
    rimmed = extended(volume, (("depth", 1),), 1)
    empty_sum = jnp.zeros((chan_local, slab_depth * cell_count), jnp.float32)
    per_plane = tap_columns(rimmed)
    flat_filters = w_first.reshape(27 * chan_local, w_first.shape[2])
    pieces = [
        lax.dot_general(
            flat_filters, plane_cols, (((0,), (0,)), ((), ())), preferred_element_type=jnp.float32
        )
        for plane_cols in per_plane
    ]
    first_sum = lax.psum_scatter(
        jnp.stack(pieces, 1).reshape(chan_local * lax.axis_size("chan"), slab_depth * cell_count),
        "chan",
        scatter_dimension=0,
        tiled=True,
    )
    hidden = jnp.maximum(first_sum + b_first[:, None], 0.0).astype(jnp.bfloat16)
    hidden = hidden.reshape(chan_local, slab_depth, cell_count)
    hidden_rim = extended(hidden, (("depth", 1),), 1)
    second_sum = fold_planes(
        w_second, empty_sum, lax.all_gather(hidden_rim, "chan", axis=0, tiled=True)
    )
    block_out = (second_sum + b_second[:, None]).astype(jnp.bfloat16)
    return block_out.reshape(chan_local, slab_depth, cell_count)


def solution(mesh):
    in_specs = (
        P("chan", "depth", None),
        P(None, "chan", None),
        P("chan"),
        P(None, None, "chan"),
        P("chan"),
    )
    out_specs = P("chan", "depth", None)
    return jax.shard_map(body, mesh=mesh, in_specs=in_specs, out_specs=out_specs, check_vma=False)
```

profile of v0, /device:TPU:1, one launch (start us, length us, event | category | flops | bytes accessed | tf_op | source)
XLA Modules:
  0.0 243.7 jit_solution(11958815443732724612)
XLA Ops:
  6.5 5.8 %collective-permute-start = (bf16[16,1,4096]{2,0,1:T(8,128)(2,1)}, bf16[16,1,4096]{2,0,1:T(8,128)(2,1)S(1)}, u32[]{:S(2)}, u32[]{:S(2)}) collective-permute-start(bf16[16,1,4096]{2,0,1:T(8,128)(2,1)} %param.5), channel_id=1, source_target_pairs={{0,16},{16,32},{32,48},{48,64},{64,80},{80,96},{96,112},{112,128},... | collective-permute-start | bytes 393224 | tf_op jit(solution)/shard_map/ppermute | solution.py:16
  12.4 1.3 collective-permute-start.1
  13.7 1.1 collective-permute-done
  14.9 10.2 %collective-permute-done.1 = bf16[16,1,4096]{2,0,1:T(8,128)(2,1)S(1)} collective-permute-done((bf16[16,1,4096]{2,0,1:T(8,128)(2,1)}, bf16[16,1,4096]{2,0,1:T(8,128)(2,1)S(1)}, u32[]{:S(2)}, u32[]{:S(2)}) %collective-permute-start.1) | collective-permute-done | bytes 131104 | tf_op jit(solution)/shard_map/ppermute | solution.py:17
  25.0 1.1 fusion.30
  26.3 0.1 fusion.69
  26.4 0.1 fusion.67
  26.5 0.1 fusion.65
  26.8 0.1 fusion.60
  27.0 0.1 fusion.55
  27.1 0.1 fusion.53
  27.3 0.1 fusion.51
  27.8 0.1 fusion.41
  27.9 0.1 fusion.39
  28.0 0.1 fusion.37
  28.4 3.4 %convolution_bitcast_fusion = f32[256,4096]{0,1:T(8,128)} fusion(bf16[432,4096]{1,0:T(8,128)(2,1)S(1)} %fusion.32, bf16[432,256]{1,0:T(8,128)(2,1)S(1)} %bitcast.261), kind=kOutput, calls=%fused_computation | convolution fusion | flops 905969664 | bytes 7954432 | tf_op jit(solution)/shard_map/dot_general | solution.py:91
  31.8 5.7 %copy.15 = f32[256,4096]{1,0:T(8,128)} copy(f32[256,4096]{0,1:T(8,128)} %convolution_bitcast_fusion) | data formatting | bytes 8388608
  37.5 70.7 %reduce-scatter.4.cloned.1.call-done = f32[16,4096]{1,0:T(8,128)} async-done(((f32[256,4096]{1,0:T(8,128)}), f32[16,4096]{1,0:T(8,128)}) %reduce-scatter.4.cloned.1.call-update) | async-done | bytes 262160
  108.2 1.5 copy.16
  109.8 0.2 fusion.24
  110.0 0.3 copy.9
  110.4 4.4 %collective-permute-start.2 = (bf16[16,1,4096]{2,0,1:T(8,128)(2,1)S(1)}, bf16[16,1,4096]{2,0,1:T(8,128)(2,1)S(1)}, u32[]{:S(2)}, u32[]{:S(2)}) collective-permute-start(bf16[16,1,4096]{2,0,1:T(8,128)(2,1)S(1)} %copy.9), channel_id=1, source_target_pairs={{0,16},{16,32},{32,48},{48,64},{64,80},{80,96},{96,112},{112,128},... | collective-permute-start | bytes 393224 | tf_op jit(solution)/shard_map/ppermute | solution.py:16
  114.7 1.5 collective-permute-start.3
  116.2 0.5 collective-permute-done.2
  116.7 6.5 %collective-permute-done.3 = bf16[16,1,4096]{2,0,1:T(8,128)(2,1)S(1)} collective-permute-done((bf16[16,1,4096]{2,0,1:T(8,128)(2,1)S(1)}, bf16[16,1,4096]{2,0,1:T(8,128)(2,1)S(1)}, u32[]{:S(2)}, u32[]{:S(2)}) %collective-permute-start.3) | collective-permute-done | bytes 131104 | tf_op jit(solution)/shard_map/ppermute | solution.py:17
  123.2 0.8 pad_maximum_fusion
  124.0 1.0 slice_bitcast_fusion.27
  125.0 43.9 %all-gather.2.cloned.1.call-done = bf16[256,3,4096]{2,0,1:T(8,128)(2,1)} async-done(((bf16[16,3,4096]{2,0,1:T(8,128)(2,1)}), bf16[256,3,4096]{2,0,1:T(8,128)(2,1)}) %all-gather.2.cloned.1.call-update) | async-done | bytes 6291472 | tf_op jit(solution)/shard_map/all_gather | solution.py:106
  168.9 2.6 %fusion.11 = bf16[2304,4096]{1,0:T(8,128)(2,1)S(1)} fusion(pred[4096]{0:T(1024)(128)(4,1)S(1)} %fusion.76, bf16[256,3,4096]{2,0,1:T(8,128)(2,1)} %all-gather.2.cloned.1.call-done), kind=kLoop, calls=%fused_computation.25 | loop fusion | flops 1048575 | bytes 8392704
  171.5 0.8 copy-done.2
  172.3 0.9 bitcast_dynamic-update-slice_fusion.1
  173.2 1.2 fusion.10
  174.4 3.2 %fusion.9 = (bf16[2304,4096]{1,0:T(8,128)(2,1)S(1)}, bf16[2304,4096]{1,0:T(8,128)(2,1)}) fusion(bf16[2304,4096]{1,0:T(8,128)(2,1)S(1)} %fusion.10, pred[4096]{0:T(1024)(128)(4,1)S(1)} %fusion.76, bf16[256,3,4096]{2,0,1:T(8,128)(2,1)S(1)} %copy-done.2), kind=kLoop, calls=%fused_computation.20 | loop fusion | flops 2097151 | bytes 10489856
  177.6 2.4 fusion.3
  180.0 3.7 %fusion.8 = (bf16[2304,4096]{1,0:T(8,128)(2,1)S(1)}, bf16[2304,4096]{1,0:T(8,128)(2,1)}) fusion(bf16[2304,4096]{1,0:T(8,128)(2,1)S(1)} %get-tuple-element.22, pred[4096]{0:T(1024)(128)(4,1)S(1)} %fusion.75, bf16[256,3,4096]{2,0,1:T(8,128)(2,1)S(1)} %copy-done.2, bf16[2304,4096]{1,0:T(8,128)(2,1)} %get-tuple-element.23), kind=kLoop, calls=%fused_computation.18 | loop fusion | flops 2097152 | bytes 10489856
  183.7 6.5 %copy-done.3 = bf16[2304,4096]{1,0:T(8,128)(2,1)} copy-done((bf16[2304,4096]{1,0:T(8,128)(2,1)}, bf16[2304,4096]{1,0:T(8,128)(2,1)S(1)}, u32[]{:S(2)}) %copy-start.3) | copy-done | bytes 18874392
  190.1 4.0 %fusion.7 = (bf16[2304,4096]{1,0:T(8,128)(2,1)}, bf16[2304,4096]{1,0:T(8,128)(2,1)}, bf16[2304,4096]{1,0:T(8,128)(2,1)S(1)}) fusion(bf16[2304,4096]{1,0:T(8,128)(2,1)} %copy-done.3, pred[4096]{0:T(1024)(128)(4,1)S(1)} %fusion.76, bf16[256,3,4096]{2,0,1:T(8,128)(2,1)S(1)} %copy-done.2, bf16[2304,4096]{1,0:T(8,128)(2,1)} %get-tuple-element.12), kind=kLoop, calls=%fused_computation.16 | loop fusion | flops 3145727 | bytes 12587008
  194.1 3.2 %bitcast_dynamic-update-slice_fusion = (bf16[2304,4096]{1,0:T(8,128)(2,1)}, bf16[2304,4096]{1,0:T(8,128)(2,1)S(1)}, bf16[2304,4096]{1,0:T(8,128)(2,1)}) fusion(bf16[2304,4096]{1,0:T(8,128)(2,1)} %get-tuple-element.8, bf16[256,3,4096]{2,0,1:T(8,128)(2,1)S(1)} %copy-done.2, bf16[2304,4096]{1,0:T(8,128)(2,1)S(1)} %get-tuple-element.10, ...), kind=kLoop, calls=%fused_computation.14 | loop fusion | bytes 14680064
  197.3 4.9 %fusion.6 = (bf16[2304,4096]{1,0:T(8,128)(2,1)}, bf16[2304,4096]{1,0:T(8,128)(2,1)}, bf16[2304,4096]{1,0:T(8,128)(2,1)S(1)}) fusion(bf16[2304,4096]{1,0:T(8,128)(2,1)} %get-tuple-element.19, pred[4096]{0:T(1024)(128)(4,1)S(1)} %fusion.75, bf16[256,3,4096]{2,0,1:T(8,128)(2,1)S(1)} %copy-done.2, bf16[2304,4096]{1,0:T(8,128)(2,1)} %get-tuple-element.21, ...), kind=kLoop, calls=%fused_computation.13 | loop fusion | flops 3145728 | bytes 12587008 | tf_op jit(solution)/shard_map/concatenate | solution.py:44
  202.2 1.2 fusion.15
  203.4 0.2 fusion.4
  203.6 1.2 fusion.14
  204.8 3.9 %fusion.13 = (bf16[2304,4096]{1,0:T(8,128)(2,1)S(1)}, bf16[2304,4096]{1,0:T(8,128)(2,1)}) fusion(bf16[2304,4096]{1,0:T(8,128)(2,1)S(1)} %fusion.14, pred[4096]{0:T(1024)(128)(4,1)S(1)} %fusion.76, bf16[256,3,4096]{2,0,1:T(8,128)(2,1)S(1)} %copy-done.2, bf16[2304,4096]{1,0:T(8,128)(2,1)} %get-tuple-element.6), kind=kLoop, calls=%fused_computation.30 | loop fusion | flops 2097152 | bytes 10489856
  208.7 4.1 %bitcast_dynamic-update-slice_fusion.2 = (bf16[2304,4096]{1,0:T(8,128)(2,1)S(1)}, bf16[2304,4096]{1,0:T(8,128)(2,1)}) fusion(bf16[2304,4096]{1,0:T(8,128)(2,1)S(1)} %get-tuple-element.17, bf16[256,3,4096]{2,0,1:T(8,128)(2,1)S(1)} %copy-done.2, bf16[2304,4096]{1,0:T(8,128)(2,1)} %get-tuple-element.18), kind=kLoop, calls=%fused_computation.28 | loop fusion | bytes 10485760
  212.8 3.9 %fusion.12 = (bf16[2304,4096]{1,0:T(8,128)(2,1)S(1)}, bf16[2304,4096]{1,0:T(8,128)(2,1)}) fusion(bf16[2304,4096]{1,0:T(8,128)(2,1)S(1)} %get-tuple-element.24, pred[4096]{0:T(1024)(128)(4,1)S(1)} %fusion.75, bf16[256,3,4096]{2,0,1:T(8,128)(2,1)S(1)} %copy-done.2, bf16[2304,4096]{1,0:T(8,128)(2,1)} %get-tuple-element.25), kind=kLoop, calls=%fused_computation.27 | loop fusion | flops 2097152 | bytes 10489856 | tf_op jit(solution)/shard_map/concatenate | solution.py:44
  216.7 7.9 %fusion.78 = f32[4096,16]{0,1:T(8,128)S(1)} fusion(bf16[2304,16]{0,1:T(8,128)(2,1)S(1)} %bitcast.264, bf16[2304,4096]{1,0:T(8,128)(2,1)} %get-tuple-element.16), kind=kOutput, calls=%fused_computation.144 | convolution fusion | flops 301989888 | bytes 19210240 | tf_op jit(solution)/shard_map/dot_general | solution.py:57
  224.6 2.6 %convolution_add_fusion.1 = f32[4096,16]{0,1:T(8,128)S(1)} fusion(f32[4096,16]{0,1:T(8,128)S(1)} %fusion.78, bf16[2304,16]{0,1:T(8,128)(2,1)S(1)} %bitcast.263, bf16[2304,4096]{1,0:T(8,128)(2,1)S(1)} %get-tuple-element.15), kind=kOutput, calls=%fused_computation.3 | convolution fusion | flops 302055424 | bytes 19472384 | tf_op jit(solution)/shard_map/dot_general | solution.py:57
  227.2 9.6 %fusion.2 = bf16[16,1,4096]{2,0,1:T(8,128)(2,1)} fusion(f32[4096,16]{0,1:T(8,128)S(1)} %convolution_add_fusion.1, bf16[2304,16]{0,1:T(8,128)(2,1)S(1)} %bitcast.262, bf16[2304,4096]{1,0:T(8,128)(2,1)} %get-tuple-element.5, f32[16]{0:T(128)S(1)} %copy-done.5), kind=kOutput, calls=%fused_computation.5 | convolution fusion | flops 302186496 | bytes 19341376 | tf_op jit(solution)/shard_map/dot_general | solution.py:57
  (38 shorter events, 1.2 us)
Async XLA Ops:
  6.5 21.9 %copy-start = (bf16[27,16,256]{2,1,0:T(8,128)(2,1)S(1)}, bf16[27,16,256]{2,1,0:T(8,128)(2,1)}, u32[]{:S(2)}) copy-start(bf16[27,16,256]{2,1,0:T(8,128)(2,1)} %param.6) | copy-start | bytes 663556
  6.5 20.7 %copy-start.4 = (bf16[16,1,4096]{2,0,1:T(8,128)(2,1)S(1)}, bf16[16,1,4096]{2,0,1:T(8,128)(2,1)}, u32[]{:S(2)}) copy-start(bf16[16,1,4096]{2,0,1:T(8,128)(2,1)} %param.5) | copy-start | bytes 393220
  6.5 101.7 %reduce-scatter.4.cloned.1.call-start = ((), (), s32[]{:S(2)}) async-start(), calls=%async_computation.2 | async-start | bytes 4456448
  6.5 8.3 %collective-permute-start = (bf16[16,1,4096]{2,0,1:T(8,128)(2,1)}, bf16[16,1,4096]{2,0,1:T(8,128)(2,1)S(1)}, u32[]{:S(2)}, u32[]{:S(2)}) collective-permute-start(bf16[16,1,4096]{2,0,1:T(8,128)(2,1)} %param.5), channel_id=1, source_target_pairs={{0,16},{16,32},{32,48},{48,64},{64,80},{80,96},{96,112},{112,128},... | collective-permute-start | bytes 393224 | tf_op jit(solution)/shard_map/ppermute | solution.py:16
  12.4 12.6 %collective-permute-start.1 = (bf16[16,1,4096]{2,0,1:T(8,128)(2,1)}, bf16[16,1,4096]{2,0,1:T(8,128)(2,1)S(1)}, u32[]{:S(2)}, u32[]{:S(2)}) collective-permute-start(bf16[16,1,4096]{2,0,1:T(8,128)(2,1)} %param.5), channel_id=1, source_target_pairs={{16,0},{32,16},{48,32},{64,48},{80,64},{96,80},{112,96},{128,112},... | collective-permute-start | bytes 393224 | tf_op jit(solution)/shard_map/ppermute | solution.py:17
  37.5 72.3 %copy-start.6 = (f32[16]{0:T(128)S(1)}, f32[16]{0:T(128)}, u32[]{:S(2)}) copy-start(f32[16]{0:T(128)} %param.7) | copy-start | bytes 196
  37.5 131.4 %all-gather.2.cloned.1.call-start = ((), (), s32[]{:S(2)}) async-start(), calls=%async_computation.1 | async-start | bytes 6684672 | tf_op jit(solution)/shard_map/all_gather | solution.py:106
  110.4 6.3 %collective-permute-start.2 = (bf16[16,1,4096]{2,0,1:T(8,128)(2,1)S(1)}, bf16[16,1,4096]{2,0,1:T(8,128)(2,1)S(1)}, u32[]{:S(2)}, u32[]{:S(2)}) collective-permute-start(bf16[16,1,4096]{2,0,1:T(8,128)(2,1)S(1)} %copy.9), channel_id=1, source_target_pairs={{0,16},{16,32},{32,48},{48,64},{64,80},{80,96},{96,112},{112,128},... | collective-permute-start | bytes 393224 | tf_op jit(solution)/shard_map/ppermute | solution.py:16
  114.7 8.5 %collective-permute-start.3 = (bf16[16,1,4096]{2,0,1:T(8,128)(2,1)S(1)}, bf16[16,1,4096]{2,0,1:T(8,128)(2,1)S(1)}, u32[]{:S(2)}, u32[]{:S(2)}) collective-permute-start(bf16[16,1,4096]{2,0,1:T(8,128)(2,1)S(1)} %copy.9), channel_id=1, source_target_pairs={{16,0},{32,16},{48,32},{64,48},{80,64},{96,80},{112,96},{128,112},... | collective-permute-start | bytes 393224 | tf_op jit(solution)/shard_map/ppermute | solution.py:17
  168.9 3.4 %copy-start.2 = (bf16[256,3,4096]{2,0,1:T(8,128)(2,1)S(1)}, bf16[256,3,4096]{2,0,1:T(8,128)(2,1)}, u32[]{:S(2)}) copy-start(bf16[256,3,4096]{2,0,1:T(8,128)(2,1)} %all-gather.2.cloned.1.call-done) | copy-start | bytes 18874372
  183.7 6.5 %copy-start.3 = (bf16[2304,4096]{1,0:T(8,128)(2,1)}, bf16[2304,4096]{1,0:T(8,128)(2,1)S(1)}, u32[]{:S(2)}) copy-start(bf16[2304,4096]{1,0:T(8,128)(2,1)S(1)} %get-tuple-element.11) | copy-start | bytes 56623108
  224.6 2.6 %copy-start.5 = (f32[16]{0:T(128)S(1)}, f32[16]{0:T(128)}, u32[]{:S(2)}) copy-start(f32[16]{0:T(128)} %param.9) | copy-start | bytes 196
  227.2 9.7 %copy-start.1 = (bf16[27,16,256]{2,1,0:T(8,128)(2,1)S(1)}, bf16[27,16,256]{2,1,0:T(8,128)(2,1)}, u32[]{:S(2)}) copy-start(bf16[27,16,256]{2,1,0:T(8,128)(2,1)} %param.6) | copy-start | bytes 663556
Sparse Core Ops, SparseCore 0:
  37.6 70.5 reduce-scatter.3
  124.1 44.7 all-gather.1
where the time goes:
time: 244 us
  waiting for transfers between devices  133 us (55%)
  other arithmetic  33.3 us (14%)
  local copies, waits for them, and re-layouts  27.3 us (11%)
  matrix products  23.5 us (10%)
  between operations  13.8 us (6%)
  starting transfers between devices  13 us (5%)
    unnamed x3, waiting for transfers between devices  70.7 us
    all_gather x1, waiting for transfers between devices, body(): lax.all_gather(hidden_rim, 'chan', axis=0, tiled=True)  43.9 us
    unnamed x31, local copies, waits for them, and re-layouts  26.9 us
    unnamed x25, other arithmetic  22.2 us
    dot_general x3, matrix products, fold_planes(): lax.dot_general(grouped[depth_tap], window, (((0,), (0,)), ((), ())), pre...  20.1 us
    ppermute x2, waiting for transfers between devices, extended(): after = lax.ppermute(leading, axis, down)  16.7 us
    ppermute x2, starting transfers between devices, extended(): before = lax.ppermute(last, axis, up)  10.2 us
    concatenate x2, other arithmetic, nine_taps(): per_plane.append(jnp.concatenate(windows, 0))  8.84 us
  transfers between devices with their start and end apart: 6, of which 6 were waited for; matrix products, arithmetic and copies ran while one was open for 0% of the time, Pallas kernels for 0%

commit v1 on v0

v1 whole, which is shorter than its diff:
```python
import jax
import jax.numpy as jnp
from jax import lax
from jax.experimental import pallas as pl
from jax.experimental.pallas import tpu as pltpu
from jax.sharding import PartitionSpec as P

W = 64


def plane_kernel(w_ref, x_ref, o_ref):
    out_chan = o_ref.shape[1]
    cell_count = x_ref.shape[1]
    x = x_ref[...]
    cell = lax.broadcasted_iota(jnp.int32, (out_chan, cell_count), 1)
    row = lax.shift_right_logical(cell, W.bit_length() - 1)
    col = cell & (W - 1)
    rows = cell_count // W
    masks = []
    for kh in range(3):
        for kw in range(3):
            ok = None
            if kh == 0:
                ok = row >= 1
            elif kh == 2:
                ok = row < rows - 1
            if kw == 0:
                ok = (col >= 1) if ok is None else ok & (col >= 1)
            elif kw == 2:
                ok = (col < W - 1) if ok is None else ok & (col < W - 1)
            masks.append(ok)
    for kd in range(3):
        z = jnp.dot(w_ref[kd], x, preferred_element_type=jnp.float32)
        acc = None
        for kh in range(3):
            for kw in range(3):
                t = kh * 3 + kw
                shift = (kh - 1) * W + (kw - 1)
                zt = z[t * out_chan : (t + 1) * out_chan]
                if shift != 0:
                    zt = pltpu.roll(zt, (-shift) % cell_count, 1)
                if masks[t] is not None:
                    zt = jnp.where(masks[t], zt, 0.0)
                acc = zt if acc is None else acc + zt
        o_ref[kd] = acc


def plane_partials(wk, x):
    out_chan = wk.shape[1] // 9
    cell_count = x.shape[1]
    return pl.pallas_call(
        plane_kernel,
        out_shape=jax.ShapeDtypeStruct((3, out_chan, cell_count), jnp.float32),
        compiler_params=pltpu.CompilerParams(vmem_limit_bytes=48 * 1024 * 1024),
    )(wk, x)


def kernel_filters(filters):
    taps, in_chan, out_chan = filters.shape
    f = filters.reshape(3, 9, in_chan, out_chan).transpose(0, 1, 3, 2)
    return f.reshape(3, 9 * out_chan, in_chan)


def depth_combine(partials):
    peers = lax.axis_size("depth")
    up = [(i, i + 1) for i in range(peers - 1)]
    down = [(j, i) for i, j in up]
    from_below = lax.ppermute(partials[-1, 0], "depth", up)
    from_above = lax.ppermute(partials[0, 2], "depth", down)
    planes = partials.shape[0]
    lower = [from_below] + [partials[p - 1, 0] for p in range(1, planes)]
    upper = [partials[p + 1, 2] for p in range(planes - 1)] + [from_above]
    return jnp.stack([partials[p, 1] + lower[p] + upper[p] for p in range(planes)], 0)


def layer(wk, source):
    planes = source.shape[1]
    partials = jnp.stack([plane_partials(wk, source[:, p]) for p in range(planes)], 0)
    return depth_combine(partials)


def body(volume, w_first, b_first, w_second, b_second):
    chan_local, slab_depth, cell_count = volume.shape
    w1 = lax.all_to_all(w_first, "chan", 2, 1, tiled=True)
    w1k = kernel_filters(w1)
    w2k = kernel_filters(w_second)
    full_volume = lax.all_gather(volume, "chan", axis=0, tiled=True)
    first_sum = layer(w1k, full_volume)
    hidden = jnp.maximum(first_sum + b_first[None, :, None], 0.0).astype(jnp.bfloat16)
    hidden = hidden.transpose(1, 0, 2)
    full_hidden = lax.all_gather(hidden, "chan", axis=0, tiled=True)
    second_sum = layer(w2k, full_hidden)
    block_out = (second_sum + b_second[None, :, None]).astype(jnp.bfloat16)
    return block_out.transpose(1, 0, 2)


def solution(mesh):
    in_specs = (
        P("chan", "depth", None),
        P(None, "chan", None),
        P("chan"),
        P(None, None, "chan"),
        P("chan"),
    )
    out_specs = P("chan", "depth", None)
    return jax.shard_map(body, mesh=mesh, in_specs=in_specs, out_specs=out_specs, check_vma=False)
```

time: 244 us -> 143 us (0.59)
  waiting for transfers between devices: 133 us -> 83.9 us
  other arithmetic: 33.3 us -> 1.49 us
  matrix products: 23.5 us -> 0 us
  blocking collectives: 0 us -> 13.8 us
  local copies, waits for them, and re-layouts: 27.3 us -> 14.8 us
  Pallas kernels: 0 us -> 4.53 us
    unnamed x3 -> x2, waiting for transfers between devices: 70.7 us -> 0.73 us
    dot_general x4 -> x0, matrix products: 23.5 us -> none  [the longest x3 20.1 us: fold_planes(): lax.dot_general(grouped[depth_tap], window, (((0,), (0,)), ((), ())), pre...]
    unnamed x25 -> x0, other arithmetic: 22.2 us -> none
    unnamed x31 -> x13, local copies, waits for them, and re-layouts: 26.9 us -> 9.67 us
    all_to_all x0 -> x1, blocking collectives: none -> 13.8 us  [body(): w1 = lax.all_to_all(w_first, 'chan', 2, 1, tiled=True)]
    ppermute x4, waiting for transfers between devices: 18.3 us -> 30.4 us  [the longest x2 21.1 us: depth_combine(): from_above = lax.ppermute(partials[0, 2], 'depth', down)]
    concatenate x5 -> x0, other arithmetic: 10.8 us -> none  [the longest x2 8.84 us: nine_taps(): per_plane.append(jnp.concatenate(windows, 0))]
    all_gather x1 -> x2, waiting for transfers between devices: 43.9 us -> 52.8 us  [the longest x1 35.6 us: body(): full_hidden = lax.all_gather(hidden, 'chan', axis=0, tiled=True)]
  transfers between devices with their start and end apart: 6 -> 6, of which waited for: 6 -> 6; matrix products, arithmetic and copies ran while one was open for 0% -> 8% of each run, Pallas kernels for 0% -> 0%
where the time goes in v1:
time: 143 us
  waiting for transfers between devices  83.9 us (59%)
  local copies, waits for them, and re-layouts  14.8 us (10%)
  blocking collectives  13.8 us (10%)
  between operations  13.5 us (9%)
  starting transfers between devices  11.2 us (8%)
  Pallas kernels  4.53 us (3%)
  other arithmetic  1.49 us (1%)
    all_gather x1, waiting for transfers between devices, body(): full_hidden = lax.all_gather(hidden, 'chan', axis=0, tiled=True)  35.6 us
    ppermute x2, waiting for transfers between devices, depth_combine(): from_above = lax.ppermute(partials[0, 2], 'depth', down)  21.1 us
    all_gather x1, waiting for transfers between devices, body(): full_volume = lax.all_gather(volume, 'chan', axis=0, tiled=True)  17.1 us
    all_to_all x1, blocking collectives, body(): w1 = lax.all_to_all(w_first, 'chan', 2, 1, tiled=True)  13.8 us
    unnamed x13, local copies, waits for them, and re-layouts  9.67 us
    ppermute x2, waiting for transfers between devices, depth_combine(): from_below = lax.ppermute(partials[-1, 0], 'depth', up)  9.3 us
    ppermute x2, starting transfers between devices, depth_combine(): from_below = lax.ppermute(partials[-1, 0], 'depth', up)  8.36 us
    pallas_call x2, Pallas kernels, plane_partials(): pl.pallas_call(plane_kernel, out_shape=jax.ShapeDtypeStruct((3, out_chan,...  4.53 us
  transfers between devices with their start and end apart: 6, of which 6 were waited for; matrix products, arithmetic and copies ran while one was open for 8% of the time, Pallas kernels for 0%

profile of v1, /device:TPU:1, one launch (start us, length us, event | category | flops | bytes accessed | tf_op | source)
XLA Modules:
  0.0 143.2 jit_solution(7568460282490048256)
XLA Ops:
  6.5 0.0 all-gather.4.cloned.1.call-start
  6.5 0.7 all-gather.4.cloned.1.call-update
  7.3 0.0 all-gather.6.cloned.1.call-start
  7.3 2.0 %copy.11 = bf16[27,16,256]{0,1,2:T(8,128)(2,1)S(1)} copy(bf16[27,16,256]{2,1,0:T(8,128)(2,1)} %param.6) | data formatting | bytes 442368 | tf_op args[1]
  9.3 1.8 %reshape.32 = bf16[16,2,3456]{2,1,0:T(2,128)(2,1)S(1)} reshape(bf16[256,16,27]{2,1,0:T(8,128)(2,1)S(1)} %bitcast.62) | data formatting | bytes 442368
  11.2 13.8 %all_to_all.15 = bf16[16,2,3456]{2,1,0:T(2,128)(2,1)S(1)} all-to-all(bf16[16,2,3456]{2,1,0:T(2,128)(2,1)S(1)} %reshape.32), channel_id=1, replica_groups=mesh['depth'=16,'chan'=16] {'chan'}, dimensions={0} | all-to-all | bytes 442368 | tf_op jit(solution)/shard_map/all_to_all | solution.py:84
  24.9 2.6 %reshape.33 = bf16[256,16,27]{2,1,0:T(8,128)(2,1)S(1)} reshape(bf16[16,2,3456]{2,1,0:T(2,128)(2,1)S(1)} %all_to_all.15) | data formatting | bytes 442368
  27.6 3.4 %copy.13 = bf16[27,16,16,16]{2,1,3,0:T(8,128)(2,1)S(1)} copy(bf16[27,16,16,16]{0,2,3,1:T(8,128)(2,1)S(1)} %bitcast.63) | data formatting | bytes 442368 | tf_op jit(solution)/shard_map/all_to_all | solution.py:84
  31.0 1.6 %reshape.28 = bf16[3,9,256,16]{2,3,1,0:T(8,128)(2,1)S(1)} reshape(bf16[27,16,16,16]{2,1,3,0:T(8,128)(2,1)S(1)} %copy.13) | data formatting | bytes 442368 | tf_op jit(solution)/shard_map/reshape | solution.py:60
  32.7 0.0 copy-start.3
  32.7 17.1 %all-gather.4.cloned.1.call-done = bf16[256,1,4096]{2,0,1:T(8,128)(2,1)} async-done(((bf16[16,1,4096]{2,0,1:T(8,128)(2,1)}), bf16[256,1,4096]{2,0,1:T(8,128)(2,1)}) %all-gather.4.cloned.1.call-update) | async-done | bytes 2097168 | tf_op jit(solution)/shard_map/all_gather | solution.py:87
  49.8 0.0 copy-start
  49.8 1.6 %copy-done = bf16[256,1,4096]{2,0,1:T(8,128)(2,1)S(1)} copy-done((bf16[256,1,4096]{2,0,1:T(8,128)(2,1)S(1)}, bf16[256,1,4096]{2,0,1:T(8,128)(2,1)}, u32[]{:S(2)}) %copy-start) | copy-done | bytes 2097176
  51.4 0.0 copy-start.2
  51.4 2.2 %shard_map.55 = f32[3,16,4096]{2,1,0:T(8,128)S(1)} custom-call(bf16[3,144,256]{2,1,0:T(8,128)(2,1)S(1)} %bitcast.60, bf16[256,4096]{1,0:T(8,128)(2,1)S(1)} %bitcast.59), custom_call_target="tpu_custom_call" | custom-call | tf_op jit(solution)/shard_map/pallas_call | solution.py:51
  53.7 4.2 %collective-permute-start = (f32[16,4096]{1,0:T(8,128)S(1)}, f32[16,4096]{1,0:T(8,128)S(1)}, u32[]{:S(2)}, u32[]{:S(2)}) collective-permute-start(f32[16,4096]{1,0:T(8,128)S(1)} %get-tuple-element.7), channel_id=1, source_target_pairs={{0,16},{16,32},{32,48},{48,64},{64,80},{80,96},{96,112},{112,128},... | collective-permute-start | bytes 786440 | tf_op jit(solution)/shard_map/ppermute | solution.py:68
  57.9 1.5 %collective-permute-start.1 = (f32[16,4096]{1,0:T(8,128)S(1)}, f32[16,4096]{1,0:T(8,128)S(1)}, u32[]{:S(2)}, u32[]{:S(2)}) collective-permute-start(f32[16,4096]{1,0:T(8,128)S(1)} %get-tuple-element.8), channel_id=1, source_target_pairs={{16,0},{32,16},{48,32},{64,48},{80,64},{96,80},{112,96},{128,112},... | collective-permute-start | bytes 786440 | tf_op jit(solution)/shard_map/ppermute | solution.py:69
  59.4 4.6 %collective-permute-done = f32[16,4096]{1,0:T(8,128)S(1)} collective-permute-done((f32[16,4096]{1,0:T(8,128)S(1)}, f32[16,4096]{1,0:T(8,128)S(1)}, u32[]{:S(2)}, u32[]{:S(2)}) %collective-permute-start) | collective-permute-done | bytes 262176 | tf_op jit(solution)/shard_map/ppermute | solution.py:68
  63.9 10.6 %collective-permute-done.1 = f32[16,4096]{1,0:T(8,128)S(1)} collective-permute-done((f32[16,4096]{1,0:T(8,128)S(1)}, f32[16,4096]{1,0:T(8,128)S(1)}, u32[]{:S(2)}, u32[]{:S(2)}) %collective-permute-start.1) | collective-permute-done | bytes 262176 | tf_op jit(solution)/shard_map/ppermute | solution.py:69
  74.6 0.0 copy-done.3
  74.6 0.7 fusion.8
  75.3 0.0 all-gather.6.cloned.1.call-update
  75.3 0.0 copy-start.4
  75.3 35.6 %all-gather.6.cloned.1.call-done.x_ref = bf16[256,4096]{1,0:T(8,128)(2,1)} async-done(((bf16[16,4096]{1,0:T(8,128)(2,1)}), bf16[256,4096]{1,0:T(8,128)(2,1)}) %all-gather.6.cloned.1.call-update) | async-done | bytes 2097168 | tf_op jit(solution)/shard_map/all_gather | solution.py:91
  111.0 0.0 copy-done.2
  111.0 0.0 copy-start.1
  111.0 1.6 %copy-done.1 = bf16[256,4096]{1,0:T(8,128)(2,1)S(1)} copy-done((bf16[256,4096]{1,0:T(8,128)(2,1)S(1)}, bf16[256,4096]{1,0:T(8,128)(2,1)}, u32[]{:S(2)}) %copy-start.1) | copy-done | bytes 2097176
  112.6 2.3 %shard_map.56 = f32[3,16,4096]{2,1,0:T(8,128)S(1)} custom-call(bf16[3,144,256]{2,1,0:T(8,128)(2,1)S(1)} %bitcast.61, bf16[256,4096]{1,0:T(8,128)(2,1)S(1)} %copy-done.1), custom_call_target="tpu_custom_call" | custom-call | tf_op jit(solution)/shard_map/pallas_call | solution.py:51
  114.9 4.2 %collective-permute-start.2 = (f32[16,4096]{1,0:T(8,128)S(1)}, f32[16,4096]{1,0:T(8,128)S(1)}, u32[]{:S(2)}, u32[]{:S(2)}) collective-permute-start(f32[16,4096]{1,0:T(8,128)S(1)} %get-tuple-element.5), channel_id=1, source_target_pairs={{0,16},{16,32},{32,48},{48,64},{64,80},{80,96},{96,112},{112,128},... | collective-permute-start | bytes 786440 | tf_op jit(solution)/shard_map/ppermute | solution.py:68
  119.1 1.3 collective-permute-start.3
  120.4 4.7 %collective-permute-done.2 = f32[16,4096]{1,0:T(8,128)S(1)} collective-permute-done((f32[16,4096]{1,0:T(8,128)S(1)}, f32[16,4096]{1,0:T(8,128)S(1)}, u32[]{:S(2)}, u32[]{:S(2)}) %collective-permute-start.2) | collective-permute-done | bytes 262176 | tf_op jit(solution)/shard_map/ppermute | solution.py:68
  125.1 10.5 %collective-permute-done.3 = f32[16,4096]{1,0:T(8,128)S(1)} collective-permute-done((f32[16,4096]{1,0:T(8,128)S(1)}, f32[16,4096]{1,0:T(8,128)S(1)}, u32[]{:S(2)}, u32[]{:S(2)}) %collective-permute-start.3) | collective-permute-done | bytes 262176 | tf_op jit(solution)/shard_map/ppermute | solution.py:69
  135.6 0.0 copy-done.4
  135.6 0.7 fusion.9
  (2 shorter events, 0.1 us)
Async XLA Ops:
  6.5 43.3 %all-gather.4.cloned.1.call-start = ((), (), s32[]{:S(2)}) async-start(), calls=%async_computation.1 | async-start | bytes 2228224 | tf_op jit(solution)/shard_map/all_gather | solution.py:87
  7.3 103.7 %all-gather.6.cloned.1.call-start = ((), (), s32[]{:S(2)}) async-start(), calls=%async_computation.2 | async-start | bytes 2228224 | tf_op jit(solution)/shard_map/all_gather | solution.py:91
  32.7 41.9 %copy-start.3 = (f32[16]{0:T(128)S(1)}, f32[16]{0:T(128)}, u32[]{:S(2)}) copy-start(f32[16]{0:T(128)} %param.7) | copy-start | bytes 196
  49.8 1.6 %copy-start = (bf16[256,1,4096]{2,0,1:T(8,128)(2,1)S(1)}, bf16[256,1,4096]{2,0,1:T(8,128)(2,1)}, u32[]{:S(2)}) copy-start(bf16[256,1,4096]{2,0,1:T(8,128)(2,1)} %all-gather.4.cloned.1.call-done) | copy-start | bytes 6291460
  51.4 59.6 %copy-start.2 = (bf16[27,256,16]{1,2,0:T(8,128)(2,1)S(1)}, bf16[27,256,16]{1,2,0:T(8,128)(2,1)}, u32[]{:S(2)}) copy-start(bf16[27,256,16]{1,2,0:T(8,128)(2,1)} %param.8) | copy-start | bytes 663556
  53.7 10.2 %collective-permute-start = (f32[16,4096]{1,0:T(8,128)S(1)}, f32[16,4096]{1,0:T(8,128)S(1)}, u32[]{:S(2)}, u32[]{:S(2)}) collective-permute-start(f32[16,4096]{1,0:T(8,128)S(1)} %get-tuple-element.7), channel_id=1, source_target_pairs={{0,16},{16,32},{32,48},{48,64},{64,80},{80,96},{96,112},{112,128},... | collective-permute-start | bytes 786440 | tf_op jit(solution)/shard_map/ppermute | solution.py:68
  57.9 16.7 %collective-permute-start.1 = (f32[16,4096]{1,0:T(8,128)S(1)}, f32[16,4096]{1,0:T(8,128)S(1)}, u32[]{:S(2)}, u32[]{:S(2)}) collective-permute-start(f32[16,4096]{1,0:T(8,128)S(1)} %get-tuple-element.8), channel_id=1, source_target_pairs={{16,0},{32,16},{48,32},{64,48},{80,64},{96,80},{112,96},{128,112},... | collective-permute-start | bytes 786440 | tf_op jit(solution)/shard_map/ppermute | solution.py:69
  75.3 60.3 %copy-start.4 = (f32[16]{0:T(128)S(1)}, f32[16]{0:T(128)}, u32[]{:S(2)}) copy-start(f32[16]{0:T(128)} %param.9) | copy-start | bytes 196
  111.0 1.6 %copy-start.1 = (bf16[256,4096]{1,0:T(8,128)(2,1)S(1)}, bf16[256,4096]{1,0:T(8,128)(2,1)}, u32[]{:S(2)}) copy-start(bf16[256,4096]{1,0:T(8,128)(2,1)} %all-gather.6.cloned.1.call-done.x_ref) | copy-start | bytes 6291460
  114.9 10.2 %collective-permute-start.2 = (f32[16,4096]{1,0:T(8,128)S(1)}, f32[16,4096]{1,0:T(8,128)S(1)}, u32[]{:S(2)}, u32[]{:S(2)}) collective-permute-start(f32[16,4096]{1,0:T(8,128)S(1)} %get-tuple-element.5), channel_id=1, source_target_pairs={{0,16},{16,32},{32,48},{48,64},{64,80},{80,96},{96,112},{112,128},... | collective-permute-start | bytes 786440 | tf_op jit(solution)/shard_map/ppermute | solution.py:68
  119.1 16.5 %collective-permute-start.3 = (f32[16,4096]{1,0:T(8,128)S(1)}, f32[16,4096]{1,0:T(8,128)S(1)}, u32[]{:S(2)}, u32[]{:S(2)}) collective-permute-start(f32[16,4096]{1,0:T(8,128)S(1)} %get-tuple-element.6), channel_id=1, source_target_pairs={{16,0},{32,16},{48,32},{64,48},{80,64},{96,80},{112,96},{128,112},... | collective-permute-start | bytes 786440 | tf_op jit(solution)/shard_map/ppermute | solution.py:69
Sparse Core Ops, SparseCore 0:
  9.2 40.5 all-gather.3
  75.5 35.4 all-gather.5

commit v2 on v1

--- a/solution.py
+++ b/solution.py
@@ -79,16 +79,34 @@
     return depth_combine(partials)
 
 
+def gather_chan(local, extra=None):
+    peers = lax.axis_size("chan")
+    flat = local.reshape(1, -1)
+    sent = jnp.broadcast_to(flat, (peers, flat.shape[1]))
+    if extra is not None:
+        sent = jnp.concatenate([sent, extra.astype(sent.dtype)], 1)
+    got = lax.all_to_all(sent, "chan", 0, 0, tiled=True)
+    full = got[:, : flat.shape[1]].reshape((peers * local.shape[0],) + local.shape[1:])
+    return full, got[:, flat.shape[1] :]
+
+
 def body(volume, w_first, b_first, w_second, b_second):
     chan_local, slab_depth, cell_count = volume.shape
-    w1 = lax.all_to_all(w_first, "chan", 2, 1, tiled=True)
-    w1k = kernel_filters(w1)
+    peers = lax.axis_size("chan")
+    taps, in_local, out_chan = w_first.shape
+    out_local = out_chan // peers
+    w_parts = w_first.reshape(3, 9, in_local, peers, out_local).transpose(3, 0, 1, 4, 2)
+    full_volume, w_got = gather_chan(volume, w_parts.reshape(peers, -1))
+    w1k = (
+        w_got.reshape(peers, 3, 9, out_local, in_local)
+        .transpose(1, 2, 3, 0, 4)
+        .reshape(3, 9 * out_local, peers * in_local)
+    )
     w2k = kernel_filters(w_second)
-    full_volume = lax.all_gather(volume, "chan", axis=0, tiled=True)
     first_sum = layer(w1k, full_volume)
     hidden = jnp.maximum(first_sum + b_first[None, :, None], 0.0).astype(jnp.bfloat16)
     hidden = hidden.transpose(1, 0, 2)
-    full_hidden = lax.all_gather(hidden, "chan", axis=0, tiled=True)
+    full_hidden, _ = gather_chan(hidden)
     second_sum = layer(w2k, full_hidden)
     block_out = (second_sum + b_second[None, :, None]).astype(jnp.bfloat16)
     return block_out.transpose(1, 0, 2)

time: 143 us -> 202 us (1.41)
  waiting for transfers between devices: 83.9 us -> 29 us
  blocking collectives: 13.8 us -> 67.6 us
  local copies, waits for them, and re-layouts: 14.8 us -> 55.5 us
  other arithmetic: 1.49 us -> 30.8 us
  between operations: 13.5 us -> 0.19 us
    all_to_all x1 -> x2, blocking collectives: 13.8 us -> 67.6 us  [gather_chan(): got = lax.all_to_all(sent, 'chan', 0, 0, tiled=True)]
    all_gather x2 -> x0, waiting for transfers between devices: 52.8 us -> none  [the longest x1 35.6 us: body(): full_hidden = lax.all_gather(hidden, 'chan', axis=0, tiled=True)]
    unnamed x13, local copies, waits for them, and re-layouts: 9.67 us -> 28.7 us
    all_to_all x0 -> x3, other arithmetic: none -> 16.9 us  [gather_chan(): got = lax.all_to_all(sent, 'chan', 0, 0, tiled=True)]
    broadcast_in_dim x0 -> x1, other arithmetic: none -> 13 us  [gather_chan(): sent = jnp.broadcast_to(flat, (peers, flat.shape[1]))]
    reshape x1 -> x6, local copies, waits for them, and re-layouts: 1.65 us -> 14.2 us  [the longest x2 5.7 us: body(): w_got.reshape(peers, 3, 9, out_local, in_local).transpose(1, 2, 3, 0, 4)]
    broadcast_in_dim x0 -> x1, local copies, waits for them, and re-layouts: none -> 5.17 us  [gather_chan(): sent = jnp.broadcast_to(flat, (peers, flat.shape[1]))]
    another operation x0 -> x2, local copies, waits for them, and re-layouts: none -> 4.45 us  [layer(): source[:, p]]
  transfers between devices with their start and end apart: 6 -> 4, of which waited for: 6 -> 4; matrix products, arithmetic and copies ran while one was open for 8% -> 0% of each run, Pallas kernels for 0% -> 0%
where the time goes in v2:
time: 202 us; the launch traced here: 201 us
  blocking collectives  67.6 us (33%)
  local copies, waits for them, and re-layouts  55.5 us (27%)
  other arithmetic  30.8 us (15%)
  waiting for transfers between devices  29 us (14%)
  starting transfers between devices  13.1 us (6%)
  Pallas kernels  4.49 us (2%)
    all_to_all x2, blocking collectives, gather_chan(): got = lax.all_to_all(sent, 'chan', 0, 0, tiled=True)  67.6 us
    unnamed x13, local copies, waits for them, and re-layouts  28.7 us
    ppermute x2, waiting for transfers between devices, depth_combine(): from_above = lax.ppermute(partials[0, 2], 'depth', down)  21.9 us
    all_to_all x3, other arithmetic, gather_chan(): got = lax.all_to_all(sent, 'chan', 0, 0, tiled=True)  16.9 us
    broadcast_in_dim x1, other arithmetic, gather_chan(): sent = jnp.broadcast_to(flat, (peers, flat.shape[1]))  13 us
    ppermute x2, starting transfers between devices, depth_combine(): from_below = lax.ppermute(partials[-1, 0], 'depth', up)  10.3 us
    ppermute x2, waiting for transfers between devices, depth_combine(): from_below = lax.ppermute(partials[-1, 0], 'depth', up)  7.07 us
    reshape x2, local copies, waits for them, and re-layouts, body(): w_got.reshape(peers, 3, 9, out_local, in_local).transpose(1, 2, 3, 0, 4)  5.7 us
  transfers between devices with their start and end apart: 4, of which 4 were waited for; matrix products, arithmetic and copies ran while one was open for 0% of the time, Pallas kernels for 0%

profile of v2, /device:TPU:1, one launch (start us, length us, event | category | flops | bytes accessed | tf_op | source)
XLA Modules:
  0.0 200.7 jit_solution(5525333438241931713)
XLA Ops:
  0.0 1.6 copy.14
  1.6 2.2 %reshape.46 = bf16[3,9,16,16,16]{4,3,2,1,0:T(8,128)(2,1)S(1)} reshape(bf16[27,16,256]{2,1,0:T(8,128)(2,1)} %param.6) | data formatting | bytes 442368 | tf_op jit(solution)/shard_map/reshape | solution.py:98
  3.8 1.9 copy.10
  5.7 1.6 reshape.47
  7.3 0.9 pad.clone
  8.3 0.2 maximum_bitcast_fusion
  8.4 0.5 broadcast.13
  9.0 3.1 %reduce.1 = bf16[16,72448]{1,0:T(8,128)(2,1)} reduce(bf16[16,1,72448]{2,0,1:T(8,128)(2,1)S(1)} %maximum_bitcast_fusion, bf16[]{:T(256)} %broadcast.13), dimensions={1}, to_apply=%copy.11.reduce_sub_computation | reduce | bytes 4636674 | tf_op jit(solution)/shard_map/all_to_all | solution.py:88
  12.0 2.0 reshape.52
  14.0 36.4 %all_to_all.18 = bf16[16,2,36224]{2,1,0:T(2,128)(2,1)} all-to-all(bf16[16,2,36224]{2,1,0:T(2,128)(2,1)S(1)} %reshape.52), channel_id=1, replica_groups=mesh['depth'=16,'chan'=16] {'chan'}, dimensions={0} | all-to-all | bytes 4636672 | tf_op jit(solution)/shard_map/all_to_all | solution.py:88
  50.4 13.0 %reshape.53 = bf16[16,1,72448]{2,1,0:T(2,128)(2,1)} reshape(bf16[16,2,36224]{2,1,0:T(2,128)(2,1)} %all_to_all.18) | data formatting | bytes 4636672
  63.3 2.6 %copy.18 = bf16[16,1,72448]{2,0,1:T(8,128)(2,1)S(1)} copy(bf16[16,1,72448]{2,1,0:T(2,128)(2,1)} %reshape.53) | data formatting | bytes 4636672
  65.9 1.5 slice.33
  67.4 2.2 %squeeze_reshape.6.x_ref = bf16[256,4096]{1,0:T(8,128)(2,1)S(1)} reshape(bf16[16,65536]{1,0:T(8,128)(2,1)} %slice.33) | data formatting | bytes 4194304 | tf_op jit(solution)/shard_map/squeeze;reshape | solution.py:78
  69.6 2.6 %reshape.48 = bf16[16,3,9,16,16]{4,3,2,1,0:T(8,128)(2,1)} reshape(bf16[16,6912]{1,0:T(8,128)(2,1)S(1)} %slice.32) | data formatting | bytes 442368 | tf_op jit(solution)/shard_map/reshape | solution.py:101
  72.2 3.1 %copy.19 = bf16[16,3,9,16,16]{4,0,3,2,1:T(8,128)(2,1)} copy(bf16[16,3,9,16,16]{4,3,2,1,0:T(8,128)(2,1)} %reshape.48) | data formatting | bytes 442368 | tf_op jit(solution)/shard_map/reshape | solution.py:101
  75.3 2.8 %reshape.49.w_ref = bf16[3,144,256]{2,1,0:T(8,128)(2,1)S(1)} reshape(bf16[3,9,16,16,16]{4,3,2,1,0:T(8,128)(2,1)} %bitcast.70) | data formatting | bytes 442368 | tf_op jit(solution)/shard_map/reshape | solution.py:103
  78.1 0.0 copy-start.1
  78.1 2.2 %shard_map.55 = f32[3,16,4096]{2,1,0:T(8,128)S(1)} custom-call(bf16[3,144,256]{2,1,0:T(8,128)(2,1)S(1)} %reshape.49.w_ref, bf16[256,4096]{1,0:T(8,128)(2,1)S(1)} %squeeze_reshape.6.x_ref), custom_call_target="tpu_custom_call" | custom-call | tf_op jit(solution)/shard_map/pallas_call | solution.py:51
  80.4 4.9 %collective-permute-start = (f32[16,4096]{1,0:T(8,128)S(1)}, f32[16,4096]{1,0:T(8,128)S(1)}, u32[]{:S(2)}, u32[]{:S(2)}) collective-permute-start(f32[16,4096]{1,0:T(8,128)S(1)} %get-tuple-element.7), channel_id=1, source_target_pairs={{0,16},{16,32},{32,48},{48,64},{64,80},{80,96},{96,112},{112,128},... | collective-permute-start | bytes 786440 | tf_op jit(solution)/shard_map/ppermute | solution.py:68
  85.3 1.5 collective-permute-start.1
  86.8 3.8 %collective-permute-done = f32[16,4096]{1,0:T(8,128)S(1)} collective-permute-done((f32[16,4096]{1,0:T(8,128)S(1)}, f32[16,4096]{1,0:T(8,128)S(1)}, u32[]{:S(2)}, u32[]{:S(2)}) %collective-permute-start) | collective-permute-done | bytes 262176 | tf_op jit(solution)/shard_map/ppermute | solution.py:68
  90.7 11.6 %collective-permute-done.1 = f32[16,4096]{1,0:T(8,128)S(1)} collective-permute-done((f32[16,4096]{1,0:T(8,128)S(1)}, f32[16,4096]{1,0:T(8,128)S(1)}, u32[]{:S(2)}, u32[]{:S(2)}) %collective-permute-start.1) | collective-permute-done | bytes 262176 | tf_op jit(solution)/shard_map/ppermute | solution.py:69
  102.2 0.0 copy-done.1
  102.2 0.1 fusion.9
  102.4 5.2 %broadcast_in_dim.19 = bf16[16,1,65536]{2,1,0:T(2,128)(2,1)} broadcast(bf16[65536]{0:T(1024)(128)(2,1)S(1)} %bitcast.71), dimensions={2} | broadcast | bytes 2228224 | tf_op jit(solution)/shard_map/broadcast_in_dim | solution.py:85
  107.5 13.0 %reduce.2 = bf16[16,65536]{1,0:T(8,128)(2,1)S(1)} reduce(bf16[16,1,65536]{2,1,0:T(2,128)(2,1)} %broadcast_in_dim.19, bf16[]{:T(256)} %broadcast.13), dimensions={1}, to_apply=%broadcast_in_dim.19.reduce_sub_computation | reduce | bytes 4194306 | tf_op jit(solution)/shard_map/broadcast_in_dim | solution.py:85
  120.5 2.8 %reshape.54 = bf16[16,2,32768]{2,1,0:T(2,128)(2,1)} reshape(bf16[16,65536]{1,0:T(8,128)(2,1)S(1)} %reduce.2) | data formatting | bytes 4194304
  123.4 31.3 %all_to_all.19 = bf16[16,2,32768]{2,1,0:T(2,128)(2,1)S(1)} all-to-all(bf16[16,2,32768]{2,1,0:T(2,128)(2,1)} %reshape.54), channel_id=1, replica_groups=mesh['depth'=16,'chan'=16] {'chan'}, dimensions={0} | all-to-all | bytes 4194304 | tf_op jit(solution)/shard_map/all_to_all | solution.py:88
  154.6 6.8 %reshape.55 = bf16[16,1,65536]{2,1,0:T(2,128)(2,1)} reshape(bf16[16,2,32768]{2,1,0:T(2,128)(2,1)S(1)} %all_to_all.19) | data formatting | bytes 4194304
  161.4 13.7 %reduce = bf16[16,65536]{1,0:T(8,128)(2,1)} reduce(bf16[16,1,65536]{2,1,0:T(2,128)(2,1)} %reshape.55, bf16[]{:T(256)} %constant.3), dimensions={1}, to_apply=%all_to_all.15.reduce_sub_computation | reduce | bytes 4194306 | tf_op jit(solution)/shard_map/all_to_all | solution.py:88
  175.1 0.0 copy-start
  175.1 2.2 %squeeze_reshape.7.x_ref = bf16[256,4096]{1,0:T(8,128)(2,1)S(1)} reshape(bf16[16,65536]{1,0:T(8,128)(2,1)} %reduce) | data formatting | bytes 4194304 | tf_op jit(solution)/shard_map/squeeze;reshape | solution.py:78
  177.3 0.0 copy-start.2
  177.4 0.0 copy-done
  177.4 2.2 %shard_map.56 = f32[3,16,4096]{2,1,0:T(8,128)S(1)} custom-call(bf16[3,144,256]{2,1,0:T(8,128)(2,1)S(1)} %bitcast.66, bf16[256,4096]{1,0:T(8,128)(2,1)S(1)} %squeeze_reshape.7.x_ref), custom_call_target="tpu_custom_call" | custom-call | tf_op jit(solution)/shard_map/pallas_call | solution.py:51
  179.7 5.4 %collective-permute-start.2 = (f32[16,4096]{1,0:T(8,128)S(1)}, f32[16,4096]{1,0:T(8,128)S(1)}, u32[]{:S(2)}, u32[]{:S(2)}) collective-permute-start(f32[16,4096]{1,0:T(8,128)S(1)} %get-tuple-element.5), channel_id=1, source_target_pairs={{0,16},{16,32},{32,48},{48,64},{64,80},{80,96},{96,112},{112,128},... | collective-permute-start | bytes 786440 | tf_op jit(solution)/shard_map/ppermute | solution.py:68
  185.0 1.3 collective-permute-start.3
  186.3 3.2 %collective-permute-done.2 = f32[16,4096]{1,0:T(8,128)S(1)} collective-permute-done((f32[16,4096]{1,0:T(8,128)S(1)}, f32[16,4096]{1,0:T(8,128)S(1)}, u32[]{:S(2)}, u32[]{:S(2)}) %collective-permute-start.2) | collective-permute-done | bytes 262176 | tf_op jit(solution)/shard_map/ppermute | solution.py:68
  189.6 10.4 %collective-permute-done.3 = f32[16,4096]{1,0:T(8,128)S(1)} collective-permute-done((f32[16,4096]{1,0:T(8,128)S(1)}, f32[16,4096]{1,0:T(8,128)S(1)}, u32[]{:S(2)}, u32[]{:S(2)}) %collective-permute-start.3) | collective-permute-done | bytes 262176 | tf_op jit(solution)/shard_map/ppermute | solution.py:69
  200.0 0.0 copy-done.2
  200.0 0.7 fusion.10
  (4 shorter events, 0.1 us)
Async XLA Ops:
  78.1 24.1 %copy-start.1 = (f32[16]{0:T(128)S(1)}, f32[16]{0:T(128)}, u32[]{:S(2)}) copy-start(f32[16]{0:T(128)} %param.7) | copy-start | bytes 196
  80.4 10.3 %collective-permute-start = (f32[16,4096]{1,0:T(8,128)S(1)}, f32[16,4096]{1,0:T(8,128)S(1)}, u32[]{:S(2)}, u32[]{:S(2)}) collective-permute-start(f32[16,4096]{1,0:T(8,128)S(1)} %get-tuple-element.7), channel_id=1, source_target_pairs={{0,16},{16,32},{32,48},{48,64},{64,80},{80,96},{96,112},{112,128},... | collective-permute-start | bytes 786440 | tf_op jit(solution)/shard_map/ppermute | solution.py:68
  85.3 16.9 %collective-permute-start.1 = (f32[16,4096]{1,0:T(8,128)S(1)}, f32[16,4096]{1,0:T(8,128)S(1)}, u32[]{:S(2)}, u32[]{:S(2)}) collective-permute-start(f32[16,4096]{1,0:T(8,128)S(1)} %get-tuple-element.8), channel_id=1, source_target_pairs={{16,0},{32,16},{48,32},{64,48},{80,64},{96,80},{112,96},{128,112},... | collective-permute-start | bytes 786440 | tf_op jit(solution)/shard_map/ppermute | solution.py:69
  175.1 2.3 %copy-start = (bf16[27,256,16]{1,2,0:T(8,128)(2,1)S(1)}, bf16[27,256,16]{1,2,0:T(8,128)(2,1)}, u32[]{:S(2)}) copy-start(bf16[27,256,16]{1,2,0:T(8,128)(2,1)} %param.8) | copy-start | bytes 663556
  177.3 22.6 %copy-start.2 = (f32[16]{0:T(128)S(1)}, f32[16]{0:T(128)}, u32[]{:S(2)}) copy-start(f32[16]{0:T(128)} %param.9) | copy-start | bytes 196
  179.7 9.9 %collective-permute-start.2 = (f32[16,4096]{1,0:T(8,128)S(1)}, f32[16,4096]{1,0:T(8,128)S(1)}, u32[]{:S(2)}, u32[]{:S(2)}) collective-permute-start(f32[16,4096]{1,0:T(8,128)S(1)} %get-tuple-element.5), channel_id=1, source_target_pairs={{0,16},{16,32},{32,48},{48,64},{64,80},{80,96},{96,112},{112,128},... | collective-permute-start | bytes 786440 | tf_op jit(solution)/shard_map/ppermute | solution.py:68
  185.0 14.9 %collective-permute-start.3 = (f32[16,4096]{1,0:T(8,128)S(1)}, f32[16,4096]{1,0:T(8,128)S(1)}, u32[]{:S(2)}, u32[]{:S(2)}) collective-permute-start(f32[16,4096]{1,0:T(8,128)S(1)} %get-tuple-element.6), channel_id=1, source_target_pairs={{16,0},{32,16},{48,32},{64,48},{80,64},{96,80},{112,96},{128,112},... | collective-permute-start | bytes 786440 | tf_op jit(solution)/shard_map/ppermute | solution.py:69

commit v3 on v1

--- a/solution.py
+++ b/solution.py
@@ -79,28 +79,38 @@
     return depth_combine(partials)
 
 
+CHAN = ("chip", "core")
+
+
+def gather_chan(local):
+    pair = lax.all_gather(local, "core", axis=0, tiled=True)
+    return lax.all_gather(pair, "chip", axis=0, tiled=True)
+
+
 def body(volume, w_first, b_first, w_second, b_second):
     chan_local, slab_depth, cell_count = volume.shape
-    w1 = lax.all_to_all(w_first, "chan", 2, 1, tiled=True)
+    w1 = lax.all_to_all(w_first, CHAN, 2, 1, tiled=True)
     w1k = kernel_filters(w1)
     w2k = kernel_filters(w_second)
-    full_volume = lax.all_gather(volume, "chan", axis=0, tiled=True)
+    full_volume = gather_chan(volume)
     first_sum = layer(w1k, full_volume)
     hidden = jnp.maximum(first_sum + b_first[None, :, None], 0.0).astype(jnp.bfloat16)
     hidden = hidden.transpose(1, 0, 2)
-    full_hidden = lax.all_gather(hidden, "chan", axis=0, tiled=True)
+    full_hidden = gather_chan(hidden)
     second_sum = layer(w2k, full_hidden)
     block_out = (second_sum + b_second[None, :, None]).astype(jnp.bfloat16)
     return block_out.transpose(1, 0, 2)
 
 
 def solution(mesh):
+    depth, chan = mesh.devices.shape
+    split = jax.sharding.Mesh(mesh.devices.reshape(depth, chan // 2, 2), ("depth",) + CHAN)
     in_specs = (
-        P("chan", "depth", None),
-        P(None, "chan", None),
-        P("chan"),
-        P(None, None, "chan"),
-        P("chan"),
+        P(CHAN, "depth", None),
+        P(None, CHAN, None),
+        P(CHAN),
+        P(None, None, CHAN),
+        P(CHAN),
     )
-    out_specs = P("chan", "depth", None)
-    return jax.shard_map(body, mesh=mesh, in_specs=in_specs, out_specs=out_specs, check_vma=False)
+    out_specs = P(CHAN, "depth", None)
+    return jax.shard_map(body, mesh=split, in_specs=in_specs, out_specs=out_specs, check_vma=False)

time: 143 us -> 181 us (1.27)
  waiting for transfers between devices: 83.9 us -> 116 us
  blocking collectives: 13.8 us -> 19.7 us
    all_gather x2, waiting for transfers between devices: 52.8 us -> 84.8 us  [gather_chan(): return lax.all_gather(pair, 'chip', axis=0, tiled=True)]
    ppermute x2, waiting for transfers between devices: 9.3 us -> 19.4 us  [depth_combine(): from_below = lax.ppermute(partials[-1, 0], 'depth', up)]
    ppermute x2, waiting for transfers between devices: 21.1 us -> 11.7 us  [depth_combine(): from_above = lax.ppermute(partials[0, 2], 'depth', down)]
    all_gather x0 -> x2, blocking collectives: none -> 9.02 us  [gather_chan(): pair = lax.all_gather(local, 'core', axis=0, tiled=True)]
    all_to_all x1, blocking collectives: 13.8 us -> 10.7 us  [body(): w1 = lax.all_to_all(w_first, CHAN, 2, 1, tiled=True)]
  transfers between devices with their start and end apart: 6 -> 6, of which waited for: 6 -> 6; matrix products, arithmetic and copies ran while one was open for 8% -> 6% of each run, Pallas kernels for 0% -> 0%
where the time goes in v3:
time: 181 us; the launch traced here: 180 us
  waiting for transfers between devices  116 us (64%)
  blocking collectives  19.7 us (11%)
  local copies, waits for them, and re-layouts  14.8 us (8%)
  between operations  13.5 us (7%)
  starting transfers between devices  11 us (6%)
  Pallas kernels  4.51 us (2%)
    all_gather x2, waiting for transfers between devices, gather_chan(): return lax.all_gather(pair, 'chip', axis=0, tiled=True)  84.8 us
    ppermute x2, waiting for transfers between devices, depth_combine(): from_below = lax.ppermute(partials[-1, 0], 'depth', up)  19.4 us
    ppermute x2, waiting for transfers between devices, depth_combine(): from_above = lax.ppermute(partials[0, 2], 'depth', down)  11.7 us
    all_to_all x1, blocking collectives, body(): w1 = lax.all_to_all(w_first, CHAN, 2, 1, tiled=True)  10.7 us
    unnamed x13, local copies, waits for them, and re-layouts  9.68 us
    all_gather x2, blocking collectives, gather_chan(): pair = lax.all_gather(local, 'core', axis=0, tiled=True)  9.02 us
    ppermute x2, starting transfers between devices, depth_combine(): from_below = lax.ppermute(partials[-1, 0], 'depth', up)  8.36 us
    pallas_call x2, Pallas kernels, plane_partials(): pl.pallas_call(plane_kernel, out_shape=jax.ShapeDtypeStruct((3, out_chan,...  4.51 us
  transfers between devices with their start and end apart: 6, of which 6 were waited for; matrix products, arithmetic and copies ran while one was open for 6% of the time, Pallas kernels for 0%

profile of v3, /device:TPU:1, one launch (start us, length us, event | category | flops | bytes accessed | tf_op | source)
XLA Modules:
  0.0 180.4 jit_solution(13727564761578863887)
XLA Ops:
  6.5 0.0 all-gather.5.cloned.1.call-start
  6.5 6.6 %all_gather.12 = bf16[32,1,4096]{2,0,1:T(8,128)(2,1)} all-gather(bf16[16,1,4096]{2,0,1:T(8,128)(2,1)} %param.5), channel_id=1, replica_groups=mesh['depth'=16,'chip'=8,'core'=2] {'core'}, dimensions={0}, use_global_device_ids=true | all-gather | bytes 393216 | tf_op jit(solution)/shard_map/all_gather | solution.py:86
  13.1 0.0 all-gather.5.cloned.1.call-update
  13.1 0.0 all-gather.7.cloned.1.call-start
  13.2 2.0 %copy.11 = bf16[27,16,256]{0,1,2:T(8,128)(2,1)S(1)} copy(bf16[27,16,256]{2,1,0:T(8,128)(2,1)} %param.6) | data formatting | bytes 442368 | tf_op args[1]
  15.2 1.8 %reshape.33 = bf16[16,2,3456]{2,1,0:T(2,128)(2,1)S(1)} reshape(bf16[256,16,27]{2,1,0:T(8,128)(2,1)S(1)} %bitcast.62) | data formatting | bytes 442368
  17.1 10.7 %all_to_all.15 = bf16[16,2,3456]{2,1,0:T(2,128)(2,1)S(1)} all-to-all(bf16[16,2,3456]{2,1,0:T(2,128)(2,1)S(1)} %reshape.33), channel_id=1, replica_groups=mesh['depth'=16,'chip'=8,'core'=2] {'chip','core'}, dimensions={0} | all-to-all | bytes 442368 | tf_op jit(solution)/shard_map/all_to_all | solution.py:92
  27.8 2.6 %reshape.34 = bf16[256,16,27]{2,1,0:T(8,128)(2,1)S(1)} reshape(bf16[16,2,3456]{2,1,0:T(2,128)(2,1)S(1)} %all_to_all.15) | data formatting | bytes 442368
  30.4 3.4 %copy.13 = bf16[27,16,16,16]{2,1,3,0:T(8,128)(2,1)S(1)} copy(bf16[27,16,16,16]{0,2,3,1:T(8,128)(2,1)S(1)} %bitcast.63) | data formatting | bytes 442368 | tf_op jit(solution)/shard_map/all_to_all | solution.py:92
  33.9 1.6 reshape.28
  35.5 0.0 copy-start.3
  35.5 32.5 %all-gather.5.cloned.1.call-done = bf16[256,1,4096]{2,0,1:T(8,128)(2,1)} async-done(((bf16[32,1,4096]{2,0,1:T(8,128)(2,1)}), bf16[256,1,4096]{2,0,1:T(8,128)(2,1)}) %all-gather.5.cloned.1.call-update) | async-done | bytes 2097168 | tf_op jit(solution)/shard_map/all_gather | solution.py:87
  68.0 0.0 copy-start
  68.0 1.6 copy-done
  69.6 0.0 copy-start.2
  69.6 2.2 %shard_map.55 = f32[3,16,4096]{2,1,0:T(8,128)S(1)} custom-call(bf16[3,144,256]{2,1,0:T(8,128)(2,1)S(1)} %bitcast.60, bf16[256,4096]{1,0:T(8,128)(2,1)S(1)} %bitcast.59), custom_call_target="tpu_custom_call" | custom-call | tf_op jit(solution)/shard_map/pallas_call | solution.py:51
  71.9 4.2 %collective-permute-start = (f32[16,4096]{1,0:T(8,128)S(1)}, f32[16,4096]{1,0:T(8,128)S(1)}, u32[]{:S(2)}, u32[]{:S(2)}) collective-permute-start(f32[16,4096]{1,0:T(8,128)S(1)} %get-tuple-element.7), channel_id=1, source_target_pairs={{0,16},{16,32},{32,48},{48,64},{64,80},{80,96},{96,112},{112,128},... | collective-permute-start | bytes 786440 | tf_op jit(solution)/shard_map/ppermute | solution.py:68
  76.1 1.3 collective-permute-start.1
  77.4 9.9 %collective-permute-done = f32[16,4096]{1,0:T(8,128)S(1)} collective-permute-done((f32[16,4096]{1,0:T(8,128)S(1)}, f32[16,4096]{1,0:T(8,128)S(1)}, u32[]{:S(2)}, u32[]{:S(2)}) %collective-permute-start) | collective-permute-done | bytes 262176 | tf_op jit(solution)/shard_map/ppermute | solution.py:68
  87.3 5.9 %collective-permute-done.1 = f32[16,4096]{1,0:T(8,128)S(1)} collective-permute-done((f32[16,4096]{1,0:T(8,128)S(1)}, f32[16,4096]{1,0:T(8,128)S(1)}, u32[]{:S(2)}, u32[]{:S(2)}) %collective-permute-start.1) | collective-permute-done | bytes 262176 | tf_op jit(solution)/shard_map/ppermute | solution.py:69
  93.2 0.0 copy-done.3
  93.2 0.1 fusion.8
  93.3 2.4 %all-gather = bf16[32,4096]{1,0:T(8,128)(2,1)} all-gather(bf16[16,4096]{1,0:T(8,128)(2,1)S(1)} %fusion.8), channel_id=2, replica_groups=mesh['depth'=16,'chip'=8,'core'=2] {'core'}, dimensions={0}, use_global_device_ids=true | all-gather | bytes 393216 | tf_op jit(solution)/shard_map/all_gather | solution.py:86
  95.7 0.0 all-gather.7.cloned.1.call-update
  95.7 0.0 copy-start.4
  95.7 52.3 %all-gather.7.cloned.1.call-done.x_ref = bf16[256,4096]{1,0:T(8,128)(2,1)} async-done(((bf16[32,4096]{1,0:T(8,128)(2,1)}), bf16[256,4096]{1,0:T(8,128)(2,1)}) %all-gather.7.cloned.1.call-update) | async-done | bytes 2097168 | tf_op jit(solution)/shard_map/all_gather | solution.py:87
  148.1 0.0 copy-done.2
  148.1 0.0 copy-start.1
  148.1 1.6 copy-done.1
  149.7 2.3 %shard_map.56 = f32[3,16,4096]{2,1,0:T(8,128)S(1)} custom-call(bf16[3,144,256]{2,1,0:T(8,128)(2,1)S(1)} %bitcast.61, bf16[256,4096]{1,0:T(8,128)(2,1)S(1)} %copy-done.1), custom_call_target="tpu_custom_call" | custom-call | tf_op jit(solution)/shard_map/pallas_call | solution.py:51
  152.0 4.2 %collective-permute-start.2 = (f32[16,4096]{1,0:T(8,128)S(1)}, f32[16,4096]{1,0:T(8,128)S(1)}, u32[]{:S(2)}, u32[]{:S(2)}) collective-permute-start(f32[16,4096]{1,0:T(8,128)S(1)} %get-tuple-element.5), channel_id=1, source_target_pairs={{0,16},{16,32},{32,48},{48,64},{64,80},{80,96},{96,112},{112,128},... | collective-permute-start | bytes 786440 | tf_op jit(solution)/shard_map/ppermute | solution.py:68
  156.2 1.3 collective-permute-start.3
  157.5 9.5 %collective-permute-done.2 = f32[16,4096]{1,0:T(8,128)S(1)} collective-permute-done((f32[16,4096]{1,0:T(8,128)S(1)}, f32[16,4096]{1,0:T(8,128)S(1)}, u32[]{:S(2)}, u32[]{:S(2)}) %collective-permute-start.2) | collective-permute-done | bytes 262176 | tf_op jit(solution)/shard_map/ppermute | solution.py:68
  166.9 5.8 %collective-permute-done.3 = f32[16,4096]{1,0:T(8,128)S(1)} collective-permute-done((f32[16,4096]{1,0:T(8,128)S(1)}, f32[16,4096]{1,0:T(8,128)S(1)}, u32[]{:S(2)}, u32[]{:S(2)}) %collective-permute-start.3) | collective-permute-done | bytes 262176 | tf_op jit(solution)/shard_map/ppermute | solution.py:69
  172.8 0.0 copy-done.4
  172.8 0.7 fusion.9
  (2 shorter events, 0.1 us)
Async XLA Ops:
  6.5 61.5 %all-gather.5.cloned.1.call-start = ((), (), s32[]{:S(2)}) async-start(), calls=%async_computation.1 | async-start | bytes 2359296 | tf_op jit(solution)/shard_map/all_gather | solution.py:87
  13.1 134.9 %all-gather.7.cloned.1.call-start = ((), (), s32[]{:S(2)}) async-start(), calls=%async_computation.2 | async-start | bytes 2359296 | tf_op jit(solution)/shard_map/all_gather | solution.py:87
  35.5 57.7 %copy-start.3 = (f32[16]{0:T(128)S(1)}, f32[16]{0:T(128)}, u32[]{:S(2)}) copy-start(f32[16]{0:T(128)} %param.7) | copy-start | bytes 196
  68.0 1.6 copy-start
  69.6 78.5 %copy-start.2 = (bf16[27,256,16]{1,2,0:T(8,128)(2,1)S(1)}, bf16[27,256,16]{1,2,0:T(8,128)(2,1)}, u32[]{:S(2)}) copy-start(bf16[27,256,16]{1,2,0:T(8,128)(2,1)} %param.8) | copy-start | bytes 663556
  71.9 15.4 %collective-permute-start = (f32[16,4096]{1,0:T(8,128)S(1)}, f32[16,4096]{1,0:T(8,128)S(1)}, u32[]{:S(2)}, u32[]{:S(2)}) collective-permute-start(f32[16,4096]{1,0:T(8,128)S(1)} %get-tuple-element.7), channel_id=1, source_target_pairs={{0,16},{16,32},{32,48},{48,64},{64,80},{80,96},{96,112},{112,128},... | collective-permute-start | bytes 786440 | tf_op jit(solution)/shard_map/ppermute | solution.py:68
  76.1 17.1 %collective-permute-start.1 = (f32[16,4096]{1,0:T(8,128)S(1)}, f32[16,4096]{1,0:T(8,128)S(1)}, u32[]{:S(2)}, u32[]{:S(2)}) collective-permute-start(f32[16,4096]{1,0:T(8,128)S(1)} %get-tuple-element.8), channel_id=1, source_target_pairs={{16,0},{32,16},{48,32},{64,48},{80,64},{96,80},{112,96},{128,112},... | collective-permute-start | bytes 786440 | tf_op jit(solution)/shard_map/ppermute | solution.py:69
  95.7 77.1 %copy-start.4 = (f32[16]{0:T(128)S(1)}, f32[16]{0:T(128)}, u32[]{:S(2)}) copy-start(f32[16]{0:T(128)} %param.9) | copy-start | bytes 196
  148.1 1.6 copy-start.1
  152.0 14.9 %collective-permute-start.2 = (f32[16,4096]{1,0:T(8,128)S(1)}, f32[16,4096]{1,0:T(8,128)S(1)}, u32[]{:S(2)}, u32[]{:S(2)}) collective-permute-start(f32[16,4096]{1,0:T(8,128)S(1)} %get-tuple-element.5), channel_id=1, source_target_pairs={{0,16},{16,32},{32,48},{48,64},{64,80},{80,96},{96,112},{112,128},... | collective-permute-start | bytes 786440 | tf_op jit(solution)/shard_map/ppermute | solution.py:68
  156.2 16.6 %collective-permute-start.3 = (f32[16,4096]{1,0:T(8,128)S(1)}, f32[16,4096]{1,0:T(8,128)S(1)}, u32[]{:S(2)}, u32[]{:S(2)}) collective-permute-start(f32[16,4096]{1,0:T(8,128)S(1)} %get-tuple-element.6), channel_id=1, source_target_pairs={{16,0},{32,16},{48,32},{64,48},{80,64},{96,80},{112,96},{128,112},... | collective-permute-start | bytes 786440 | tf_op jit(solution)/shard_map/ppermute | solution.py:69
Sparse Core Ops, SparseCore 0:
  13.3 54.6 all-gather.4
  95.8 52.1 all-gather.6
